TPU v7x, 512 devices: a whole 4x4x16 slice. The times are simulated.
512 devices in a mesh: band: 8 (over x_lo, y), xy: 64 (over z, x_hi, core).
Axes of the slice: x: 4 (x_hi: 2, x_lo: 2; x = x_hi * 2 + x_lo), y: 4, z: 16, core: 2. Of those that a mesh axis runs over, the one named last changes fastest.
Arguments:
- orbitals: float32 [16, 64, 128, 256], P('band', 'xy'), may hold values from -6 to 6
- energies: float32 [16], P('band'), may hold values from -1.5 to -0.25
- occupation: int32 [16], P('band'), may hold values from 1 to 2
- potential: float32 [64, 128, 256], P('xy'), may hold values from 0.25 to 2
- trials: float32 [4, 64, 128, 256], P(None, 'xy'), may hold values from -8 to 23
Outputs:
- density: float32 [4, 64, 128, 256], P(None, 'xy', 'band')
- response_matrix: float32 [4, 4], replicated
All inputs are finite; a program needn't handle non-finite values.
Results may differ from a plain program's by a relative error of at most 0.0001.
Values sent between devices are 32-bit elements; how exact they have to be, the bound alone decides.
No kernel may reach another device: no remote copies, remote signals or barrier semaphores. Data moves between devices by JAX's collectives and lax.ppermute only.
A program may use at most 64 MiB of HBM per device.

v0:
```python
import math
import jax
import jax.numpy as jnp
from jax import lax
from jax.sharding import PartitionSpec as P

ITERS = 3


def padded_2(block, sides, width):
    for axis, dim in sides:
        count = lax.axis_size(axis)
        forward = [(i, i + 1) for i in range(count - 1)]
        forward.append((count - 1, 0))
        backward = [(target, source) for source, target in forward]
        low = lax.ppermute(
            lax.slice_in_dim(block, block.shape[dim] - width, None, axis=dim), axis, forward
        )
        high = lax.ppermute(lax.slice_in_dim(block, 0, width, axis=dim), axis, backward)
        block = jnp.concatenate([low, block, high], axis=dim)
    return block


def respond(psi_rows, energy_rows, weight_rows, potential_part, trial_part, project, apply_op):
    orbital_count, cell_count = psi_rows.shape
    trial_count = trial_part.shape[0]
    row_count = orbital_count * trial_count
    diagonal_op = 3.0 + potential_part.reshape(1, 1, cell_count) - energy_rows[:, None, None]
    diagonal_op = jnp.broadcast_to(diagonal_op, (orbital_count, trial_count, cell_count)).reshape(
        row_count, cell_count
    )
    products = trial_part[None, :, :] * psi_rows[:, None, :]
    right_side = -project(products.reshape(row_count, cell_count))
    update = project(right_side / diagonal_op)
    for iteration in range(ITERS):
        residual = right_side - apply_op(update, diagonal_op)
        update = update + project(residual / diagonal_op)
    weights = weight_rows[:, None, None] * psi_rows[:, None, :]
    return jnp.sum(weights * update.reshape(orbital_count, trial_count, cell_count), axis=0)


def neighbours_z(field_block):
    z_padded = jnp.pad(field_block, ((0, 0), (0, 0), (0, 0), (1, 1)))
    return z_padded[..., 2:] + z_padded[..., :-2]


def local(orbitals, energies, occupation, potential, trials):
    nb_dev, width_x, width_y, width_z = orbitals.shape
    trial_count = trials.shape[0]
    cell_count = width_x * width_y * width_z
    cell_total = cell_count * lax.axis_size("xy")
    orbital_total = nb_dev * lax.axis_size("band")
    y_share = width_y // lax.axis_size("band")
    band_index = lax.axis_index("band")
    highest = lax.Precision.HIGHEST
    trial_slice = lax.dynamic_slice_in_dim(trials, band_index * y_share, y_share, 2)
    psi_flat = orbitals.reshape(nb_dev, cell_count)
    psi_all = lax.all_gather(psi_flat, "band", axis=0, tiled=True)

    def project_slab(vectors):
        intersection = jnp.dot(
            psi_all, vectors.T, precision=highest, preferred_element_type=jnp.float32
        )
        intersection = lax.psum(intersection, "xy") / cell_total
        return vectors - jnp.dot(
            intersection.T, psi_all, precision=highest, preferred_element_type=jnp.float32
        )

    def apply_slab(vectors, diagonal_op):
        field_block = vectors.reshape(-1, width_x, width_y, width_z)
        padded = padded_2(field_block, (("xy", 1),), 1)
        beside = padded[:, 2:] + padded[:, :-2]
        beside = beside + jnp.roll(field_block, 1, 2) + jnp.roll(field_block, -1, 2)
        beside = beside + neighbours_z(field_block)
        return diagonal_op * vectors - 0.5 * beside.reshape(vectors.shape)

    summed = respond(
        psi_flat,
        energies,
        occupation.astype(jnp.float32),
        potential.reshape(cell_count),
        trials.reshape(trial_count, cell_count),
        project_slab,
        apply_slab,
    )
    partial_grid = (summed / math.sqrt(orbital_total)).reshape(
        trial_count, width_x, width_y, width_z
    )
    density = lax.psum_scatter(partial_grid, "band", scatter_dimension=2, tiled=True)
    local_sum = jnp.dot(
        density.reshape(trial_count, -1),
        trial_slice.reshape(trial_count, -1).T,
        precision=highest,
        preferred_element_type=jnp.float32,
    )
    response_matrix = lax.psum(local_sum, ("band", "xy")) / cell_total
    return (density, response_matrix)


def solution(mesh):
    in_specs = (
        P("band", "xy", None, None),
        P("band"),
        P("band"),
        P("xy", None, None),
        P(None, "xy", None, None),
    )
    out_specs = (P(None, "xy", "band", None), P())
    return jax.shard_map(local, mesh=mesh, in_specs=in_specs, out_specs=out_specs, check_vma=False)
```

profile of v0, /device:TPU:1, one launch (start us, length us, event | category | flops | bytes accessed | tf_op | source)
XLA Modules:
  0.0 987.3 jit_solution(15164408557984125261)
XLA Ops:
  7.2 1.8 reshape.121
  12.4 1.4 mul.77
  13.7 45.2 %all-gather.3.cloned.1.call-done = f32[8,2,32768]{2,1,0:T(2,128)} async-done(((f32[1,2,32768]{2,1,0:T(2,128)}), f32[8,2,32768]{2,1,0:T(2,128)}) %all-gather.3.cloned.1.call-update) | async-done | bytes 2097168 | tf_op jit(solution)/shard_map/all_gather | solution.py:58
  58.9 2.7 reshape.122
  61.6 3.8 convolution_bitcast_fusion.4
  65.4 135.0 %psum.42 = f32[16,8]{0,1:T(8,128)S(1)} all-reduce(f32[16,8]{0,1:T(8,128)S(1)} %convolution_bitcast_fusion.4), channel_id=1, replica_groups=mesh['band'=8,'xy'=64] {'xy'}, use_global_device_ids=true, to_apply=%region_0.0 | all-reduce | flops 128 | bytes 1024 | tf_op jit(solution)/shard_map/psum | solution.py:64
  200.4 3.4 fusion.40
  204.8 2.5 convolution_bitcast_fusion.3
  207.4 128.3 %psum.43 = f32[16,8]{0,1:T(8,128)S(1)} all-reduce(f32[16,8]{0,1:T(8,128)S(1)} %convolution_bitcast_fusion.3), channel_id=1, replica_groups=mesh['band'=8,'xy'=64] {'xy'}, use_global_device_ids=true, to_apply=%region_1.0 | all-reduce | flops 128 | bytes 1024 | tf_op jit(solution)/shard_map/psum | solution.py:64
  335.7 2.3 convolution_subtract_fusion.3
  338.0 2.9 collective-permute-start
  340.9 4.4 collective-permute-start.1
  345.4 21.4 %collective-permute-done = f32[8,1,128,256]{3,0,2,1:T(8,128)S(1)} collective-permute-done((f32[8,1,128,256]{3,0,2,1:T(8,128)S(1)}, f32[8,1,128,256]{3,0,2,1:T(8,128)S(1)}, u32[]{:S(2)}, u32[]{:S(2)}) %collective-permute-start) | collective-permute-done | bytes 1048608 | tf_op jit(solution)/shard_map/ppermute | solution.py:19
  368.5 2.7 convolution_bitcast_fusion.2
  371.2 124.7 %psum.44 = f32[16,8]{0,1:T(8,128)S(1)} all-reduce(f32[16,8]{0,1:T(8,128)S(1)} %convolution_bitcast_fusion.2), channel_id=1, replica_groups=mesh['band'=8,'xy'=64] {'xy'}, use_global_device_ids=true, to_apply=%region_2.3 | all-reduce | flops 128 | bytes 1024 | tf_op jit(solution)/shard_map/psum | solution.py:64
  495.9 3.1 fusion.2
  499.1 6.5 collective-permute-start.2
  505.5 1.9 collective-permute-start.3
  507.7 20.3 %collective-permute-done.2 = f32[8,1,128,256]{3,0,2,1:T(8,128)S(1)} collective-permute-done((f32[8,1,128,256]{3,0,2,1:T(8,128)S(1)}, f32[8,1,128,256]{3,0,2,1:T(8,128)S(1)}, u32[]{:S(2)}, u32[]{:S(2)}) %collective-permute-start.2) | collective-permute-done | bytes 1048608 | tf_op jit(solution)/shard_map/ppermute | solution.py:19
  529.6 2.7 convolution_bitcast_fusion.1
  532.3 127.0 %psum.45 = f32[16,8]{0,1:T(8,128)S(1)} all-reduce(f32[16,8]{0,1:T(8,128)S(1)} %convolution_bitcast_fusion.1), channel_id=1, replica_groups=mesh['band'=8,'xy'=64] {'xy'}, use_global_device_ids=true, to_apply=%region_3.4 | all-reduce | flops 128 | bytes 1024 | tf_op jit(solution)/shard_map/psum | solution.py:64
  659.3 3.1 fusion.1
  662.4 4.2 collective-permute-start.4
  666.6 2.9 collective-permute-start.5
  670.5 20.8 %collective-permute-done.4 = f32[8,1,128,256]{3,0,2,1:T(8,128)S(1)} collective-permute-done((f32[8,1,128,256]{3,0,2,1:T(8,128)S(1)}, f32[8,1,128,256]{3,0,2,1:T(8,128)S(1)}, u32[]{:S(2)}, u32[]{:S(2)}) %collective-permute-start.4) | collective-permute-done | bytes 1048608 | tf_op jit(solution)/shard_map/ppermute | solution.py:19
  692.9 2.7 convolution_bitcast_fusion
  695.6 124.9 %psum.46 = f32[16,8]{0,1:T(8,128)S(1)} all-reduce(f32[16,8]{0,1:T(8,128)S(1)} %convolution_bitcast_fusion), channel_id=1, replica_groups=mesh['band'=8,'xy'=64] {'xy'}, use_global_device_ids=true, to_apply=%region_4.5 | all-reduce | flops 128 | bytes 1024 | tf_op jit(solution)/shard_map/psum | solution.py:64
  820.5 4.1 fusion
  824.7 1.6 reshape.118
  828.6 41.6 %reduce-scatter.2.cloned.1.call-done = f32[4,1,16,256]{3,2,1,0:T(8,128)} async-done(((f32[4,1,128,256]{3,2,1,0:T(8,128)}), f32[4,1,16,256]{3,2,1,0:T(8,128)}) %reduce-scatter.2.cloned.1.call-update) | async-done | bytes 65552 | tf_op jit(solution)/shard_map/reduce_scatter | solution.py:89
  870.1 1.2 convolution_bitcast_fusion.5
  871.4 108.6 %psum.47 = f32[4,4]{1,0:T(4,128)S(1)} all-reduce(f32[4,4]{1,0:T(4,128)S(1)} %convolution_bitcast_fusion.5), channel_id=1, replica_groups=mesh['band'=8,'xy'=64] {'band','xy'}, use_global_device_ids=true, to_apply=%region_7.8 | all-reduce | flops 16 | bytes 128 | tf_op jit(solution)/shard_map/psum | solution.py:96
  (59 shorter events, 13.3 us)
Async XLA Ops:
  7.2 51.8 %all-gather.3.cloned.1.call-start = ((), (), s32[]{:S(2)}) async-start(), calls=%async_computation.2 | async-start | bytes 2359296 | tf_op jit(solution)/shard_map/all_gather | solution.py:58
  9.1 861.1 %reduce-scatter.2.cloned.1.call-start = ((), (), s32[]{:S(2)}) async-start(), calls=%async_computation.1 | async-start | bytes 589824 | tf_op jit(solution)/shard_map/reduce_scatter | solution.py:89
  10.0 1.5 copy-start.11
  10.1 1.7 copy-start.12
  203.9 1.0 copy-start.6
  338.0 29.5 %copy-start.5 = (f32[8,32768]{1,0:T(8,128)}, f32[8,32768]{1,0:T(8,128)S(1)}, u32[]{:S(2)}) copy-start(f32[8,32768]{1,0:T(8,128)S(1)} %convolution_subtract_fusion.3) | copy-start | bytes 3145732
  338.0 28.9 %collective-permute-start = (f32[8,1,128,256]{3,0,2,1:T(8,128)S(1)}, f32[8,1,128,256]{3,0,2,1:T(8,128)S(1)}, u32[]{:S(2)}, u32[]{:S(2)}) collective-permute-start(f32[8,1,128,256]{3,0,2,1:T(8,128)S(1)} %bitcast.60), channel_id=1, source_target_pairs={{1,0},{2,1},{3,2},{4,3},{5,4},{6,5},{7,6},{8,7},{9,8},{10,9},{11,1... | collective-permute-start | bytes 3145736 | tf_op jit(solution)/shard_map/ppermute | solution.py:19
  340.9 26.0 %collective-permute-start.1 = (f32[8,1,128,256]{3,0,2,1:T(8,128)S(1)}, f32[8,1,128,256]{3,0,2,1:T(8,128)S(1)}, u32[]{:S(2)}, u32[]{:S(2)}) collective-permute-start(f32[8,1,128,256]{3,0,2,1:T(8,128)S(1)} %bitcast.61), channel_id=1, source_target_pairs={{0,1},{1,2},{2,3},{3,4},{4,5},{5,6},{6,7},{7,8},{8,9},{9,10},{10,1... | collective-permute-start | bytes 3145736 | tf_op jit(solution)/shard_map/ppermute | solution.py:16
  366.9 1.7 copy-start
  367.5 1.0 copy-start.8
  495.9 11.6 %copy-start.13 = (s32[2]{0:T(128)S(1)}, s32[2]{0:T(128)}, u32[]{:S(2)}) copy-start(s32[2]{0:T(128)} %param.7) | copy-start | bytes 28
  499.1 29.5 %copy-start.4 = (f32[8,32768]{1,0:T(8,128)}, f32[8,32768]{1,0:T(8,128)S(1)}, u32[]{:S(2)}) copy-start(f32[8,32768]{1,0:T(8,128)S(1)} %fusion.2) | copy-start | bytes 3145732
  499.1 28.9 %collective-permute-start.2 = (f32[8,1,128,256]{3,0,2,1:T(8,128)S(1)}, f32[8,1,128,256]{3,0,2,1:T(8,128)S(1)}, u32[]{:S(2)}, u32[]{:S(2)}) collective-permute-start(f32[8,1,128,256]{3,0,2,1:T(8,128)S(1)} %bitcast.55), channel_id=1, source_target_pairs={{1,0},{2,1},{3,2},{4,3},{5,4},{6,5},{7,6},{8,7},{9,8},{10,9},{11,1... | collective-permute-start | bytes 3145736 | tf_op jit(solution)/shard_map/ppermute | solution.py:19
  505.5 22.4 %collective-permute-start.3 = (f32[8,1,128,256]{3,0,2,1:T(8,128)S(1)}, f32[8,1,128,256]{3,0,2,1:T(8,128)S(1)}, u32[]{:S(2)}, u32[]{:S(2)}) collective-permute-start(f32[8,1,128,256]{3,0,2,1:T(8,128)S(1)} %bitcast.56), channel_id=1, source_target_pairs={{0,1},{1,2},{2,3},{3,4},{4,5},{5,6},{6,7},{7,8},{8,9},{9,10},{10,1... | collective-permute-start | bytes 3145736 | tf_op jit(solution)/shard_map/ppermute | solution.py:16
  527.9 1.7 copy-start.1
  528.6 1.0 copy-start.9
  662.4 29.5 %copy-start.3 = (f32[8,32768]{1,0:T(8,128)}, f32[8,32768]{1,0:T(8,128)S(1)}, u32[]{:S(2)}) copy-start(f32[8,32768]{1,0:T(8,128)S(1)} %fusion.1) | copy-start | bytes 3145732
  662.4 28.9 %collective-permute-start.4 = (f32[8,1,128,256]{3,0,2,1:T(8,128)S(1)}, f32[8,1,128,256]{3,0,2,1:T(8,128)S(1)}, u32[]{:S(2)}, u32[]{:S(2)}) collective-permute-start(f32[8,1,128,256]{3,0,2,1:T(8,128)S(1)} %bitcast.50), channel_id=1, source_target_pairs={{1,0},{2,1},{3,2},{4,3},{5,4},{6,5},{7,6},{8,7},{9,8},{10,9},{11,1... | collective-permute-start | bytes 3145736 | tf_op jit(solution)/shard_map/ppermute | solution.py:19
  666.6 24.7 %collective-permute-start.5 = (f32[8,1,128,256]{3,0,2,1:T(8,128)S(1)}, f32[8,1,128,256]{3,0,2,1:T(8,128)S(1)}, u32[]{:S(2)}, u32[]{:S(2)}) collective-permute-start(f32[8,1,128,256]{3,0,2,1:T(8,128)S(1)} %bitcast.51), channel_id=1, source_target_pairs={{0,1},{1,2},{2,3},{3,4},{4,5},{5,6},{6,7},{7,8},{8,9},{9,10},{10,1... | collective-permute-start | bytes 3145736 | tf_op jit(solution)/shard_map/ppermute | solution.py:16
  691.3 1.7 copy-start.2
  691.9 1.0 copy-start.7
  824.7 1.6 copy-start.10
Sparse Core Ops, SparseCore 0:
  10.0 48.8 all-gather.2
  827.8 42.2 reduce-scatter.1
where the time goes:
time: 988 us; the launch traced here: 987 us
  blocking collectives  749 us (76%)
  waiting for transfers between devices  149 us (15%)
  matrix products  31.7 us (3%)
  starting transfers between devices  22.8 us (2%)
  local copies, waits for them, and re-layouts  14.8 us (1%)
  between operations  14.4 us (1%)
    psum x5, blocking collectives, project_slab(): intersection = lax.psum(intersection, 'xy') / cell_total  640 us
    psum x1, blocking collectives, local(): response_matrix = lax.psum(local_sum, ('band', 'xy')) / cell_total  109 us
    ppermute x3, waiting for transfers between devices, padded_2(): lax.ppermute(lax.slice_in_dim(block, 0, width, axis=dim), axis, backward)  62.5 us
    all_gather x1, waiting for transfers between devices, local(): psi_all = lax.all_gather(psi_flat, 'band', axis=0, tiled=True)  45.2 us
    reduce_scatter x1, waiting for transfers between devices, local(): lax.psum_scatter(partial_grid, 'band', scatter_dimension=2, tiled=True)  41.6 us
  transfers between devices with their start and end apart: 8, of which 5 were waited for; matrix products, arithmetic and copies ran while one was open for 1% of the time, Pallas kernels for 0%

commit v1 on v0

--- a/solution.py
+++ b/solution.py
@@ -93,7 +93,7 @@
         precision=highest,
         preferred_element_type=jnp.float32,
     )
-    response_matrix = lax.psum(local_sum, ("band", "xy")) / cell_total
+    response_matrix = jnp.sum(lax.all_gather(local_sum, ("band", "xy")), axis=0) / cell_total
     return (density, response_matrix)
 
 

time: 988 us -> 1570 us (1.59)
  blocking collectives: 749 us -> 1330 us
    all_gather x0 -> x1, blocking collectives: none -> 690 us  [local(): lax.all_gather(local_sum, ('band', 'xy'))]
    psum x1 -> x0, blocking collectives: 109 us -> none  [local(): response_matrix = lax.psum(local_sum, ('band', 'xy')) / cell_total]
  transfers between devices with their start and end apart: 8 -> 8, of which waited for: 5 -> 5; matrix products, arithmetic and copies ran while one was open for 1% -> 0% of each run, Pallas kernels for 0% -> 0%
where the time goes in v1:
time: 1570 us
  blocking collectives  1330 us (85%)
  waiting for transfers between devices  149 us (9%)
  matrix products  31.7 us (2%)
  starting transfers between devices  22.8 us (1%)
    all_gather x1, blocking collectives, local(): lax.all_gather(local_sum, ('band', 'xy'))  690 us
    psum x5, blocking collectives, project_slab(): intersection = lax.psum(intersection, 'xy') / cell_total  640 us
    ppermute x3, waiting for transfers between devices, padded_2(): lax.ppermute(lax.slice_in_dim(block, 0, width, axis=dim), axis, backward)  62.5 us
    all_gather x1, waiting for transfers between devices, local(): psi_all = lax.all_gather(psi_flat, 'band', axis=0, tiled=True)  45.2 us
    reduce_scatter x1, waiting for transfers between devices, local(): lax.psum_scatter(partial_grid, 'band', scatter_dimension=2, tiled=True)  41.6 us
  transfers between devices with their start and end apart: 8, of which 5 were waited for; matrix products, arithmetic and copies ran while one was open for 0% of the time, Pallas kernels for 0%

profile of v1, /device:TPU:1, one launch (start us, length us, event | category | flops | bytes accessed | tf_op | source)
XLA Modules:
  0.0 1569.2 jit_solution(9935744630120468647)
XLA Ops:
  7.2 1.8 reshape.122
  12.4 1.4 mul.77
  13.7 45.2 %all-gather.5.cloned.1.call-done = f32[8,2,32768]{2,1,0:T(2,128)} async-done(((f32[1,2,32768]{2,1,0:T(2,128)}), f32[8,2,32768]{2,1,0:T(2,128)}) %all-gather.5.cloned.1.call-update) | async-done | bytes 2097168 | tf_op jit(solution)/shard_map/all_gather | solution.py:58
  58.9 2.7 reshape.123
  61.6 3.8 convolution_bitcast_fusion.4
  65.4 135.0 %psum.35 = f32[16,8]{0,1:T(8,128)S(1)} all-reduce(f32[16,8]{0,1:T(8,128)S(1)} %convolution_bitcast_fusion.4), channel_id=1, replica_groups=mesh['band'=8,'xy'=64] {'xy'}, use_global_device_ids=true, to_apply=%region_0.0 | all-reduce | flops 128 | bytes 1024 | tf_op jit(solution)/shard_map/psum | solution.py:64
  200.4 3.4 fusion.40
  204.8 2.5 convolution_bitcast_fusion.3
  207.4 128.3 %psum.36 = f32[16,8]{0,1:T(8,128)S(1)} all-reduce(f32[16,8]{0,1:T(8,128)S(1)} %convolution_bitcast_fusion.3), channel_id=1, replica_groups=mesh['band'=8,'xy'=64] {'xy'}, use_global_device_ids=true, to_apply=%region_1.0 | all-reduce | flops 128 | bytes 1024 | tf_op jit(solution)/shard_map/psum | solution.py:64
  335.7 2.3 convolution_subtract_fusion.3
  338.0 2.9 collective-permute-start
  340.9 4.4 collective-permute-start.1
  345.4 21.4 %collective-permute-done = f32[8,1,128,256]{3,0,2,1:T(8,128)S(1)} collective-permute-done((f32[8,1,128,256]{3,0,2,1:T(8,128)S(1)}, f32[8,1,128,256]{3,0,2,1:T(8,128)S(1)}, u32[]{:S(2)}, u32[]{:S(2)}) %collective-permute-start) | collective-permute-done | bytes 1048608 | tf_op jit(solution)/shard_map/ppermute | solution.py:19
  368.5 2.7 convolution_bitcast_fusion.2
  371.2 124.7 %psum.37 = f32[16,8]{0,1:T(8,128)S(1)} all-reduce(f32[16,8]{0,1:T(8,128)S(1)} %convolution_bitcast_fusion.2), channel_id=1, replica_groups=mesh['band'=8,'xy'=64] {'xy'}, use_global_device_ids=true, to_apply=%region_2.3 | all-reduce | flops 128 | bytes 1024 | tf_op jit(solution)/shard_map/psum | solution.py:64
  495.9 3.1 fusion.2
  499.1 6.5 collective-permute-start.2
  505.5 1.9 collective-permute-start.3
  507.7 20.3 %collective-permute-done.2 = f32[8,1,128,256]{3,0,2,1:T(8,128)S(1)} collective-permute-done((f32[8,1,128,256]{3,0,2,1:T(8,128)S(1)}, f32[8,1,128,256]{3,0,2,1:T(8,128)S(1)}, u32[]{:S(2)}, u32[]{:S(2)}) %collective-permute-start.2) | collective-permute-done | bytes 1048608 | tf_op jit(solution)/shard_map/ppermute | solution.py:19
  529.6 2.7 convolution_bitcast_fusion.1
  532.3 127.0 %psum.38 = f32[16,8]{0,1:T(8,128)S(1)} all-reduce(f32[16,8]{0,1:T(8,128)S(1)} %convolution_bitcast_fusion.1), channel_id=1, replica_groups=mesh['band'=8,'xy'=64] {'xy'}, use_global_device_ids=true, to_apply=%region_3.4 | all-reduce | flops 128 | bytes 1024 | tf_op jit(solution)/shard_map/psum | solution.py:64
  659.3 3.1 fusion.1
  662.4 4.2 collective-permute-start.4
  666.6 2.9 collective-permute-start.5
  670.5 20.8 %collective-permute-done.4 = f32[8,1,128,256]{3,0,2,1:T(8,128)S(1)} collective-permute-done((f32[8,1,128,256]{3,0,2,1:T(8,128)S(1)}, f32[8,1,128,256]{3,0,2,1:T(8,128)S(1)}, u32[]{:S(2)}, u32[]{:S(2)}) %collective-permute-start.4) | collective-permute-done | bytes 1048608 | tf_op jit(solution)/shard_map/ppermute | solution.py:19
  692.9 2.7 convolution_bitcast_fusion
  695.6 124.9 %psum.39 = f32[16,8]{0,1:T(8,128)S(1)} all-reduce(f32[16,8]{0,1:T(8,128)S(1)} %convolution_bitcast_fusion), channel_id=1, replica_groups=mesh['band'=8,'xy'=64] {'xy'}, use_global_device_ids=true, to_apply=%region_4.5 | all-reduce | flops 128 | bytes 1024 | tf_op jit(solution)/shard_map/psum | solution.py:64
  820.5 4.1 fusion
  824.7 1.6 reshape.118
  828.6 41.6 %reduce-scatter.2.cloned.1.call-done = f32[4,1,16,256]{3,2,1,0:T(8,128)} async-done(((f32[4,1,128,256]{3,2,1,0:T(8,128)}), f32[4,1,16,256]{3,2,1,0:T(8,128)}) %reduce-scatter.2.cloned.1.call-update) | async-done | bytes 65552 | tf_op jit(solution)/shard_map/reduce_scatter | solution.py:89
  870.1 1.2 convolution_bitcast_fusion.5
  871.4 689.9 %all-gather.2 = f32[512,4,4]{2,1,0:T(4,128)S(1)} all-gather(f32[1,4,4]{2,1,0:T(4,128)S(1)} %convolution_bitcast_fusion.5), channel_id=2, replica_groups=mesh['band'=8,'xy'=64] {'band','xy'}, dimensions={0}, use_global_device_ids=true | all-gather | bytes 32832 | tf_op jit(solution)/shard_map/all_gather | solution.py:96
  (60 shorter events, 13.9 us)
Async XLA Ops:
  7.2 51.8 %all-gather.5.cloned.1.call-start = ((), (), s32[]{:S(2)}) async-start(), calls=%async_computation.2 | async-start | bytes 2359296 | tf_op jit(solution)/shard_map/all_gather | solution.py:58
  9.1 861.1 %reduce-scatter.2.cloned.1.call-start = ((), (), s32[]{:S(2)}) async-start(), calls=%async_computation.1 | async-start | bytes 589824 | tf_op jit(solution)/shard_map/reduce_scatter | solution.py:89
  10.0 1.5 copy-start.11
  10.1 1.7 copy-start.12
  203.9 1.0 copy-start.6
  338.0 29.5 %copy-start.5 = (f32[8,32768]{1,0:T(8,128)}, f32[8,32768]{1,0:T(8,128)S(1)}, u32[]{:S(2)}) copy-start(f32[8,32768]{1,0:T(8,128)S(1)} %convolution_subtract_fusion.3) | copy-start | bytes 3145732
  338.0 28.9 %collective-permute-start = (f32[8,1,128,256]{3,0,2,1:T(8,128)S(1)}, f32[8,1,128,256]{3,0,2,1:T(8,128)S(1)}, u32[]{:S(2)}, u32[]{:S(2)}) collective-permute-start(f32[8,1,128,256]{3,0,2,1:T(8,128)S(1)} %bitcast.61), channel_id=1, source_target_pairs={{1,0},{2,1},{3,2},{4,3},{5,4},{6,5},{7,6},{8,7},{9,8},{10,9},{11,1... | collective-permute-start | bytes 3145736 | tf_op jit(solution)/shard_map/ppermute | solution.py:19
  340.9 26.0 %collective-permute-start.1 = (f32[8,1,128,256]{3,0,2,1:T(8,128)S(1)}, f32[8,1,128,256]{3,0,2,1:T(8,128)S(1)}, u32[]{:S(2)}, u32[]{:S(2)}) collective-permute-start(f32[8,1,128,256]{3,0,2,1:T(8,128)S(1)} %bitcast.62), channel_id=1, source_target_pairs={{0,1},{1,2},{2,3},{3,4},{4,5},{5,6},{6,7},{7,8},{8,9},{9,10},{10,1... | collective-permute-start | bytes 3145736 | tf_op jit(solution)/shard_map/ppermute | solution.py:16
  366.9 1.7 copy-start
  367.5 1.0 copy-start.8
  495.9 11.6 copy-start.13
  499.1 29.5 %copy-start.4 = (f32[8,32768]{1,0:T(8,128)}, f32[8,32768]{1,0:T(8,128)S(1)}, u32[]{:S(2)}) copy-start(f32[8,32768]{1,0:T(8,128)S(1)} %fusion.2) | copy-start | bytes 3145732
  499.1 28.9 %collective-permute-start.2 = (f32[8,1,128,256]{3,0,2,1:T(8,128)S(1)}, f32[8,1,128,256]{3,0,2,1:T(8,128)S(1)}, u32[]{:S(2)}, u32[]{:S(2)}) collective-permute-start(f32[8,1,128,256]{3,0,2,1:T(8,128)S(1)} %bitcast.56), channel_id=1, source_target_pairs={{1,0},{2,1},{3,2},{4,3},{5,4},{6,5},{7,6},{8,7},{9,8},{10,9},{11,1... | collective-permute-start | bytes 3145736 | tf_op jit(solution)/shard_map/ppermute | solution.py:19
  505.5 22.4 %collective-permute-start.3 = (f32[8,1,128,256]{3,0,2,1:T(8,128)S(1)}, f32[8,1,128,256]{3,0,2,1:T(8,128)S(1)}, u32[]{:S(2)}, u32[]{:S(2)}) collective-permute-start(f32[8,1,128,256]{3,0,2,1:T(8,128)S(1)} %bitcast.57), channel_id=1, source_target_pairs={{0,1},{1,2},{2,3},{3,4},{4,5},{5,6},{6,7},{7,8},{8,9},{9,10},{10,1... | collective-permute-start | bytes 3145736 | tf_op jit(solution)/shard_map/ppermute | solution.py:16
  527.9 1.7 copy-start.1
  528.6 1.0 copy-start.9
  662.4 29.5 %copy-start.3 = (f32[8,32768]{1,0:T(8,128)}, f32[8,32768]{1,0:T(8,128)S(1)}, u32[]{:S(2)}) copy-start(f32[8,32768]{1,0:T(8,128)S(1)} %fusion.1) | copy-start | bytes 3145732
  662.4 28.9 %collective-permute-start.4 = (f32[8,1,128,256]{3,0,2,1:T(8,128)S(1)}, f32[8,1,128,256]{3,0,2,1:T(8,128)S(1)}, u32[]{:S(2)}, u32[]{:S(2)}) collective-permute-start(f32[8,1,128,256]{3,0,2,1:T(8,128)S(1)} %bitcast.51), channel_id=1, source_target_pairs={{1,0},{2,1},{3,2},{4,3},{5,4},{6,5},{7,6},{8,7},{9,8},{10,9},{11,1... | collective-permute-start | bytes 3145736 | tf_op jit(solution)/shard_map/ppermute | solution.py:19
  666.6 24.7 %collective-permute-start.5 = (f32[8,1,128,256]{3,0,2,1:T(8,128)S(1)}, f32[8,1,128,256]{3,0,2,1:T(8,128)S(1)}, u32[]{:S(2)}, u32[]{:S(2)}) collective-permute-start(f32[8,1,128,256]{3,0,2,1:T(8,128)S(1)} %bitcast.52), channel_id=1, source_target_pairs={{0,1},{1,2},{2,3},{3,4},{4,5},{5,6},{6,7},{7,8},{8,9},{9,10},{10,1... | collective-permute-start | bytes 3145736 | tf_op jit(solution)/shard_map/ppermute | solution.py:16
  691.3 1.7 copy-start.2
  691.9 1.0 copy-start.7
  824.7 1.6 copy-start.10
Sparse Core Ops, SparseCore 0:
  10.0 48.8 all-gather.4
  827.8 42.2 reduce-scatter.1
